TPU v7x, 32 devices: a whole 2x2x4 slice. The times are simulated.
32 devices in a mesh: parts: 2 (over y), row: 2 (over x), col: 2 (over core), layer: 4 (over z).
Axes of the slice: x: 2, y: 2, z: 4, core: 2. Of those that a mesh axis runs over, the one named last changes fastest.
Arguments:
- dosages: bfloat16 [4096, 2048], P(('layer', 'col'), ('parts', 'row')), parts along dimension 1, may hold values from -6 to 6
- expression: bfloat16 [4096, 16384], P('layer', ('col', 'row')), may hold values from -6 to 6
Outputs:
- zscores: float32 [2048, 16384], P(('parts', 'row', 'layer'), 'col'), parts along dimension 0
There are 2 independent parts, one for each index of `parts`. A program takes and returns all parts, laid end to end along the dimension named above; an argument that names none is the same for every part. Nothing has to cross between parts.
All inputs are finite; a program needn't handle non-finite values.
Results may differ from a plain program's by a relative error of at most 0.0003.
Values may be sent and summed in bfloat16 or wider, within the bound.
No kernel may reach another device: no remote copies, remote signals or barrier semaphores. Data moves between devices by JAX's collectives and lax.ppermute only.
A program may use at most 128 MiB of HBM per device.

v0:
```python
import math
import jax
import jax.numpy as jnp
from jax import lax
from jax.sharding import PartitionSpec as P


def contract(left_rows, right_rows):
    return lax.dot_general(
        left_rows, right_rows, (((0,), (0,)), ((), ())), preferred_element_type=jnp.float32
    )


def full_dosages(local):
    samples = lax.all_gather(local, "col", axis=0, tiled=True)
    return lax.all_gather(samples, "row", axis=1, tiled=True)


def pick(d4, index):
    block = lax.dynamic_index_in_dim(d4, index, axis=2, keepdims=False)
    return block.reshape(block.shape[0], -1)


def on_device(dosages, expression):
    layers = lax.axis_size("layer")
    rows = lax.axis_size("row")
    layer = lax.axis_index("layer")
    row = lax.axis_index("row")
    factor = 1.0 / math.sqrt(dosages.shape[0] * lax.axis_size("col") * layers)
    samples, width = expression.shape
    block = dosages.shape[1] // layers
    half = layers // 2
    inward = [(0, 1), (layers - 1, layers - 2)]
    across = [(half - 1, half), (half, half - 1)]
    outward = [(1, 0), (layers - 2, layers - 1)]
    dosages_in = lax.ppermute(dosages, "layer", inward)
    own4 = full_dosages(dosages).reshape(samples, rows, layers, block)
    out4 = full_dosages(dosages_in).reshape(samples, rows, layers, block)
    is_left = layer < half
    outer = jnp.where(is_left, 0, layers - 1)
    near = layers - 1 - layer
    far = layers - 1 - outer
    own_far = jnp.concatenate([pick(own4, near), pick(own4, far)], axis=1)
    out_far = jnp.concatenate([pick(out4, near), pick(out4, far)], axis=1)
    own_here = pick(own4, layer)
    out_here = pick(out4, layer)
    own_outer = pick(own4, outer)
    stripe = rows * block
    chunks = max(1, min(8, width // 512))
    step = width // chunks
    output = jnp.zeros((block, rows * width), jnp.float32)
    for k in range(chunks):
        mine = expression[:, k * step : (k + 1) * step]
        theirs = lax.ppermute(mine, "layer", inward)
        sent = contract(own_far, mine) + contract(out_far, theirs)
        got = lax.ppermute(sent, "layer", across)
        to_outer = contract(own_outer, mine) + got[stripe:]
        from_inner = lax.ppermute(to_outer, "layer", outward)
        final = contract(own_here, mine) + contract(out_here, theirs) + got[:stripe] + from_inner
        final = (final * factor).reshape(rows, block, step)
        for shift in range(rows):
            target = (row + shift) % rows
            piece = lax.dynamic_index_in_dim(final, target, axis=0, keepdims=False)
            if shift:
                pairs = [(source, (source + shift) % rows) for source in range(rows)]
                piece = lax.ppermute(piece, "row", pairs)
            source = (row - shift) % rows
            output = lax.dynamic_update_slice_in_dim(output, piece, source * width + k * step, 1)
    return output


def solution(mesh):
    return jax.shard_map(
        on_device,
        mesh=mesh,
        in_specs=(P(("layer", "col"), ("parts", "row")), P("layer", ("col", "row"))),
        out_specs=P(("parts", "row", "layer"), "col"),
        check_vma=False,
    )
```

profile of v0, /device:TPU:0, one launch (start us, length us, event | category | flops | bytes accessed | tf_op | source)
XLA Modules:
  0.0 399.0 jit_solution(11919725374042339640)
XLA Ops:
  6.5 2.0 copy.3
  8.7 5.0 %collective-permute-start = (bf16[512,512]{0,1:T(8,128)(2,1)}, bf16[512,512]{0,1:T(8,128)(2,1)S(1)}, u32[]{:S(2)}, u32[]{:S(2)}) collective-permute-start(bf16[512,512]{0,1:T(8,128)(2,1)} %copy.3), channel_id=1, source_target_pairs={{0,1},{3,2},{4,5},{7,6},{8,9},{11,10},{12,13},{15,14},{16,17},{19,... | collective-permute-start | bytes 1572872 | tf_op jit(solution)/shard_map/ppermute | solution.py:36
  13.7 11.4 %collective-permute-done = bf16[512,512]{0,1:T(8,128)(2,1)S(1)} collective-permute-done((bf16[512,512]{0,1:T(8,128)(2,1)}, bf16[512,512]{0,1:T(8,128)(2,1)S(1)}, u32[]{:S(2)}, u32[]{:S(2)}) %collective-permute-start) | collective-permute-done | bytes 524320 | tf_op jit(solution)/shard_map/ppermute | solution.py:36
  26.7 9.4 %all-gather.9.cloned.1.call-done = bf16[1024,512]{0,1:T(8,128)(2,1)} async-done(((bf16[512,512]{0,1:T(8,128)(2,1)}), bf16[1024,512]{0,1:T(8,128)(2,1)}) %all-gather.9.cloned.1.call-update) | async-done | bytes 1048592 | tf_op jit(solution)/shard_map/all_gather | solution.py:15
  36.2 6.3 %fusion.88 = (bf16[1024,512]{1,0:T(8,128)(2,1)}, bf16[1024,512]{1,0:T(8,128)(2,1)}, bf16[1024,512]{1,0:T(8,128)(2,1)}, bf16[1024,512]{1,0:T(8,128)(2,1)}, bf16[1...) fusion(bf16[1024,4096]{1,0:T(8,128)(2,1)} %param.3), kind=kLoop, calls=%fused_computation.129 | loop fusion | bytes 16777216 | tf_op jit(solution)/shard_map/slice | solution.py:53
  42.4 3.7 collective-permute-start.21
  47.5 2.3 collective-permute-start.13
  51.1 2.3 collective-permute-start.5
  53.4 18.5 %all-gather.7.cloned.1.call-done = bf16[1024,1024]{0,1:T(8,128)(2,1)} async-done(((bf16[1024,512]{0,1:T(8,128)(2,1)}), bf16[1024,1024]{0,1:T(8,128)(2,1)}) %all-gather.7.cloned.1.call-update) | async-done | bytes 2097168 | tf_op jit(solution)/shard_map/all_gather | solution.py:16
  72.0 34.5 %all-gather.11.cloned.1.call-done = bf16[1024,1024]{0,1:T(8,128)(2,1)} async-done(((bf16[1024,512]{0,1:T(8,128)(2,1)}), bf16[1024,1024]{0,1:T(8,128)(2,1)}) %all-gather.11.cloned.1.call-update) | async-done | bytes 2097168 | tf_op jit(solution)/shard_map/all_gather | solution.py:16
  106.5 2.6 constant_dynamic-slice_fusion.5
  109.1 2.1 fusion.42
  111.2 1.9 fusion.50
  116.4 3.4 collective-permute-start.1
  124.1 1.9 convolution_add_fusion.4
  126.0 11.3 %collective-permute-done.9 = bf16[1024,512]{1,0:T(8,128)(2,1)S(1)} collective-permute-done((bf16[1024,512]{1,0:T(8,128)(2,1)}, bf16[1024,512]{1,0:T(8,128)(2,1)S(1)}, u32[]{:S(2)}, u32[]{:S(2)}) %collective-permute-start.9) | collective-permute-done | bytes 1048608 | tf_op jit(solution)/shard_map/ppermute | solution.py:54
  141.7 18.2 %collective-permute-done.5 = bf16[1024,512]{1,0:T(8,128)(2,1)} collective-permute-done((bf16[1024,512]{1,0:T(8,128)(2,1)}, bf16[1024,512]{1,0:T(8,128)(2,1)}, u32[]{:S(2)}, u32[]{:S(2)}) %collective-permute-start.5) | collective-permute-done | bytes 1048608 | tf_op jit(solution)/shard_map/ppermute | solution.py:54
  160.6 1.9 convolution_add_fusion.6
  162.5 19.7 %collective-permute-done.1 = bf16[1024,512]{1,0:T(8,128)(2,1)S(1)} collective-permute-done((bf16[1024,512]{1,0:T(8,128)(2,1)S(1)}, bf16[1024,512]{1,0:T(8,128)(2,1)S(1)}, u32[]{:S(2)}, u32[]{:S(2)}) %collective-permute-start.1) | collective-permute-done | bytes 1048608 | tf_op jit(solution)/shard_map/ppermute | solution.py:54
  183.6 21.0 %collective-permute-done.25 = bf16[1024,512]{1,0:T(8,128)(2,1)S(1)} collective-permute-done((bf16[1024,512]{1,0:T(8,128)(2,1)S(1)}, bf16[1024,512]{1,0:T(8,128)(2,1)S(1)}, u32[]{:S(2)}, u32[]{:S(2)}) %collective-permute-start.25) | collective-permute-done | bytes 1048608 | tf_op jit(solution)/shard_map/ppermute | solution.py:54
  206.3 20.2 %collective-permute-done.29 = bf16[1024,512]{1,0:T(8,128)(2,1)S(1)} collective-permute-done((bf16[1024,512]{1,0:T(8,128)(2,1)S(1)}, bf16[1024,512]{1,0:T(8,128)(2,1)S(1)}, u32[]{:S(2)}, u32[]{:S(2)}) %collective-permute-start.29) | collective-permute-done | bytes 1048608 | tf_op jit(solution)/shard_map/ppermute | solution.py:54
  242.1 70.3 %collective-permute-done.7 = f32[256,512]{1,0:T(8,128)S(1)} collective-permute-done((f32[256,512]{1,0:T(8,128)S(1)}, f32[256,512]{1,0:T(8,128)S(1)}, u32[]{:S(2)}, u32[]{:S(2)}) %collective-permute-start.7) | collective-permute-done | bytes 524320 | tf_op jit(solution)/shard_map/ppermute | solution.py:58
  313.7 1.7 fusion.21
  315.4 21.5 %collective-permute-done.3 = f32[256,512]{1,0:T(8,128)S(1)} collective-permute-done((f32[256,512]{1,0:T(8,128)S(1)}, f32[256,512]{1,0:T(8,128)S(1)}, u32[]{:S(2)}, u32[]{:S(2)}) %collective-permute-start.3) | collective-permute-done | bytes 524320 | tf_op jit(solution)/shard_map/ppermute | solution.py:58
  340.0 1.7 fusion.17
  341.7 6.4 %collective-permute-done.11 = f32[256,512]{1,0:T(8,128)S(1)} collective-permute-done((f32[256,512]{1,0:T(8,128)S(1)}, f32[256,512]{1,0:T(8,128)S(1)}, u32[]{:S(2)}, u32[]{:S(2)}) %collective-permute-start.11) | collective-permute-done | bytes 524320 | tf_op jit(solution)/shard_map/ppermute | solution.py:58
  353.4 6.0 %collective-permute-done.27 = f32[256,512]{1,0:T(8,128)S(1)} collective-permute-done((f32[256,512]{1,0:T(8,128)S(1)}, f32[256,512]{1,0:T(8,128)S(1)}, u32[]{:S(2)}, u32[]{:S(2)}) %collective-permute-start.27) | collective-permute-done | bytes 524320 | tf_op jit(solution)/shard_map/ppermute | solution.py:58
  361.3 7.3 %collective-permute-done.31 = f32[256,512]{1,0:T(8,128)S(1)} collective-permute-done((f32[256,512]{1,0:T(8,128)S(1)}, f32[256,512]{1,0:T(8,128)S(1)}, u32[]{:S(2)}, u32[]{:S(2)}) %collective-permute-start.31) | collective-permute-done | bytes 524320 | tf_op jit(solution)/shard_map/ppermute | solution.py:58
  374.1 3.6 collective-permute-done.20
  377.8 5.6 %collective-permute-done.24 = f32[128,512]{1,0:T(8,128)S(1)} collective-permute-done((f32[128,512]{1,0:T(8,128)S(1)}, f32[128,512]{1,0:T(8,128)S(1)}, u32[]{:S(2)}, u32[]{:S(2)}) %collective-permute-start.24) | collective-permute-done | bytes 262176 | tf_op jit(solution)/shard_map/ppermute | solution.py:66
  383.4 5.5 %collective-permute-done.28 = f32[128,512]{1,0:T(8,128)S(1)} collective-permute-done((f32[128,512]{1,0:T(8,128)S(1)}, f32[128,512]{1,0:T(8,128)S(1)}, u32[]{:S(2)}, u32[]{:S(2)}) %collective-permute-start.28) | collective-permute-done | bytes 262176 | tf_op jit(solution)/shard_map/ppermute | solution.py:66
  389.0 2.7 collective-permute-done.32
  (129 shorter events, 52.9 us)
Async XLA Ops:
  6.5 19.4 %all-gather.5.cloned.1.call-start = ((), (), s32[]{:S(2)}) async-start(), calls=%async_computation | async-start | bytes 1572864 | tf_op jit(solution)/shard_map/all_gather | solution.py:15
  8.6 27.5 %all-gather.9.cloned.1.call-start = ((), (), s32[]{:S(2)}) async-start(), calls=%async_computation.2 | async-start | bytes 1572864 | tf_op jit(solution)/shard_map/all_gather | solution.py:15
  8.7 16.4 %collective-permute-start = (bf16[512,512]{0,1:T(8,128)(2,1)}, bf16[512,512]{0,1:T(8,128)(2,1)S(1)}, u32[]{:S(2)}, u32[]{:S(2)}) collective-permute-start(bf16[512,512]{0,1:T(8,128)(2,1)} %copy.3), channel_id=1, source_target_pairs={{0,1},{3,2},{4,5},{7,6},{8,9},{11,10},{12,13},{15,14},{16,17},{19,... | collective-permute-start | bytes 1572872 | tf_op jit(solution)/shard_map/ppermute | solution.py:36
  25.9 46.1 %all-gather.7.cloned.1.call-start = ((), (), s32[]{:S(2)}) async-start(), calls=%async_computation.1 | async-start | bytes 3145728 | tf_op jit(solution)/shard_map/all_gather | solution.py:16
  26.6 79.9 %all-gather.11.cloned.1.call-start = ((), (), s32[]{:S(2)}) async-start(), calls=%async_computation.3 | async-start | bytes 3145728 | tf_op jit(solution)/shard_map/all_gather | solution.py:16
  42.4 73.9 %collective-permute-start.21 = (bf16[1024,512]{1,0:T(8,128)(2,1)}, bf16[1024,512]{1,0:T(8,128)(2,1)S(1)}, u32[]{:S(2)}, u32[]{:S(2)}) collective-permute-start(bf16[1024,512]{1,0:T(8,128)(2,1)} %get-tuple-element.6), channel_id=1, source_target_pairs={{0,1},{3,2},{4,5},{7,6},{8,9},{11,10},{12,13},{15,14},{16,17},{19,... | collective-permute-start | bytes 3145736 | tf_op jit(solution)/shard_map/ppermute | solution.py:54
  46.2 74.4 %collective-permute-start.17 = (bf16[1024,512]{1,0:T(8,128)(2,1)}, bf16[1024,512]{1,0:T(8,128)(2,1)S(1)}, u32[]{:S(2)}, u32[]{:S(2)}) collective-permute-start(bf16[1024,512]{1,0:T(8,128)(2,1)} %get-tuple-element.7), channel_id=1, source_target_pairs={{0,1},{3,2},{4,5},{7,6},{8,9},{11,10},{12,13},{15,14},{16,17},{19,... | collective-permute-start | bytes 3145736 | tf_op jit(solution)/shard_map/ppermute | solution.py:54
  47.5 75.2 %collective-permute-start.13 = (bf16[1024,512]{1,0:T(8,128)(2,1)}, bf16[1024,512]{1,0:T(8,128)(2,1)}, u32[]{:S(2)}, u32[]{:S(2)}) collective-permute-start(bf16[1024,512]{1,0:T(8,128)(2,1)} %get-tuple-element.8), channel_id=1, source_target_pairs={{0,1},{3,2},{4,5},{7,6},{8,9},{11,10},{12,13},{15,14},{16,17},{19,... | collective-permute-start | bytes 3145736 | tf_op jit(solution)/shard_map/ppermute | solution.py:54
  49.8 87.6 %collective-permute-start.9 = (bf16[1024,512]{1,0:T(8,128)(2,1)}, bf16[1024,512]{1,0:T(8,128)(2,1)S(1)}, u32[]{:S(2)}, u32[]{:S(2)}) collective-permute-start(bf16[1024,512]{1,0:T(8,128)(2,1)} %get-tuple-element.9), channel_id=1, source_target_pairs={{0,1},{3,2},{4,5},{7,6},{8,9},{11,10},{12,13},{15,14},{16,17},{19,... | collective-permute-start | bytes 3145736 | tf_op jit(solution)/shard_map/ppermute | solution.py:54
  51.1 108.7 %collective-permute-start.5 = (bf16[1024,512]{1,0:T(8,128)(2,1)}, bf16[1024,512]{1,0:T(8,128)(2,1)}, u32[]{:S(2)}, u32[]{:S(2)}) collective-permute-start(bf16[1024,512]{1,0:T(8,128)(2,1)} %get-tuple-element.10), channel_id=1, source_target_pairs={{0,1},{3,2},{4,5},{7,6},{8,9},{11,10},{12,13},{15,14},{16,17},{19,... | collective-permute-start | bytes 3145736 | tf_op jit(solution)/shard_map/ppermute | solution.py:54
  116.4 65.8 %collective-permute-start.1 = (bf16[1024,512]{1,0:T(8,128)(2,1)S(1)}, bf16[1024,512]{1,0:T(8,128)(2,1)S(1)}, u32[]{:S(2)}, u32[]{:S(2)}) collective-permute-start(bf16[1024,512]{1,0:T(8,128)(2,1)S(1)} %copy-done.3), channel_id=1, source_target_pairs={{0,1},{3,2},{4,5},{7,6},{8,9},{11,10},{12,13},{15,14},{16,17},{19,... | collective-permute-start | bytes 3145736 | tf_op jit(solution)/shard_map/ppermute | solution.py:54
  120.6 84.1 %collective-permute-start.25 = (bf16[1024,512]{1,0:T(8,128)(2,1)S(1)}, bf16[1024,512]{1,0:T(8,128)(2,1)S(1)}, u32[]{:S(2)}, u32[]{:S(2)}) collective-permute-start(bf16[1024,512]{1,0:T(8,128)(2,1)S(1)} %copy-done.2), channel_id=1, source_target_pairs={{0,1},{3,2},{4,5},{7,6},{8,9},{11,10},{12,13},{15,14},{16,17},{19,... | collective-permute-start | bytes 3145736 | tf_op jit(solution)/shard_map/ppermute | solution.py:54
  122.7 103.7 %collective-permute-start.29 = (bf16[1024,512]{1,0:T(8,128)(2,1)S(1)}, bf16[1024,512]{1,0:T(8,128)(2,1)S(1)}, u32[]{:S(2)}, u32[]{:S(2)}) collective-permute-start(bf16[1024,512]{1,0:T(8,128)(2,1)S(1)} %copy-done.1), channel_id=1, source_target_pairs={{0,1},{3,2},{4,5},{7,6},{8,9},{11,10},{12,13},{15,14},{16,17},{19,... | collective-permute-start | bytes 3145736 | tf_op jit(solution)/shard_map/ppermute | solution.py:54
  137.4 92.3 %collective-permute-start.22 = (f32[512,512]{1,0:T(8,128)S(1)}, f32[512,512]{1,0:T(8,128)S(1)}, u32[]{:S(2)}, u32[]{:S(2)}) collective-permute-start(f32[512,512]{1,0:T(8,128)S(1)} %convolution_add_fusion.2), channel_id=1, source_target_pairs={{1,2},{2,1},{5,6},{6,5},{9,10},{10,9},{13,14},{14,13},{17,18},{18,... | collective-permute-start | bytes 3145736 | tf_op jit(solution)/shard_map/ppermute | solution.py:56
  159.8 71.1 %collective-permute-start.18 = (f32[512,512]{1,0:T(8,128)S(1)}, f32[512,512]{1,0:T(8,128)S(1)}, u32[]{:S(2)}, u32[]{:S(2)}) collective-permute-start(f32[512,512]{1,0:T(8,128)S(1)} %convolution_add_fusion.3), channel_id=1, source_target_pairs={{1,2},{2,1},{5,6},{6,5},{9,10},{10,9},{13,14},{14,13},{17,18},{18,... | collective-permute-start | bytes 3145736 | tf_op jit(solution)/shard_map/ppermute | solution.py:56
  182.2 49.9 %collective-permute-start.14 = (f32[512,512]{1,0:T(8,128)S(1)}, f32[512,512]{1,0:T(8,128)S(1)}, u32[]{:S(2)}, u32[]{:S(2)}) collective-permute-start(f32[512,512]{1,0:T(8,128)S(1)} %convolution_add_fusion.4), channel_id=1, source_target_pairs={{1,2},{2,1},{5,6},{6,5},{9,10},{10,9},{13,14},{14,13},{17,18},{18,... | collective-permute-start | bytes 3145736 | tf_op jit(solution)/shard_map/ppermute | solution.py:56
  204.7 28.6 %collective-permute-start.10 = (f32[512,512]{1,0:T(8,128)S(1)}, f32[512,512]{1,0:T(8,128)S(1)}, u32[]{:S(2)}, u32[]{:S(2)}) collective-permute-start(f32[512,512]{1,0:T(8,128)S(1)} %convolution_add_fusion.5), channel_id=1, source_target_pairs={{1,2},{2,1},{5,6},{6,5},{9,10},{10,9},{13,14},{14,13},{17,18},{18,... | collective-permute-start | bytes 3145736 | tf_op jit(solution)/shard_map/ppermute | solution.py:56
  233.3 116.9 %collective-permute-start.23 = (f32[256,512]{1,0:T(8,128)S(1)}, f32[256,512]{1,0:T(8,128)S(1)}, u32[]{:S(2)}, u32[]{:S(2)}) collective-permute-start(f32[256,512]{1,0:T(8,128)S(1)} %slice_add_fusion.2), channel_id=1, source_target_pairs={{1,0},{2,3},{5,4},{6,7},{9,8},{10,11},{13,12},{14,15},{17,16},{18,... | collective-permute-start | bytes 1572872 | tf_op jit(solution)/shard_map/ppermute | solution.py:58
  235.0 116.2 %collective-permute-start.19 = (f32[256,512]{1,0:T(8,128)S(1)}, f32[256,512]{1,0:T(8,128)S(1)}, u32[]{:S(2)}, u32[]{:S(2)}) collective-permute-start(f32[256,512]{1,0:T(8,128)S(1)} %slice_add_fusion.3), channel_id=1, source_target_pairs={{1,0},{2,3},{5,4},{6,7},{9,8},{10,11},{13,12},{14,15},{17,16},{18,... | collective-permute-start | bytes 1572872 | tf_op jit(solution)/shard_map/ppermute | solution.py:58
  236.8 101.9 %collective-permute-start.15 = (f32[256,512]{1,0:T(8,128)S(1)}, f32[256,512]{1,0:T(8,128)S(1)}, u32[]{:S(2)}, u32[]{:S(2)}) collective-permute-start(f32[256,512]{1,0:T(8,128)S(1)} %slice_add_fusion.4), channel_id=1, source_target_pairs={{1,0},{2,3},{5,4},{6,7},{9,8},{10,11},{13,12},{14,15},{17,16},{18,... | collective-permute-start | bytes 1572872 | tf_op jit(solution)/shard_map/ppermute | solution.py:58
  238.6 73.8 %collective-permute-start.7 = (f32[256,512]{1,0:T(8,128)S(1)}, f32[256,512]{1,0:T(8,128)S(1)}, u32[]{:S(2)}, u32[]{:S(2)}) collective-permute-start(f32[256,512]{1,0:T(8,128)S(1)} %slice_add_fusion.6), channel_id=1, source_target_pairs={{1,0},{2,3},{5,4},{6,7},{9,8},{10,11},{13,12},{14,15},{17,16},{18,... | collective-permute-start | bytes 1572872 | tf_op jit(solution)/shard_map/ppermute | solution.py:58
  240.3 96.6 %collective-permute-start.3 = (f32[256,512]{1,0:T(8,128)S(1)}, f32[256,512]{1,0:T(8,128)S(1)}, u32[]{:S(2)}, u32[]{:S(2)}) collective-permute-start(f32[256,512]{1,0:T(8,128)S(1)} %slice_add_fusion.7), channel_id=1, source_target_pairs={{1,0},{2,3},{5,4},{6,7},{9,8},{10,11},{13,12},{14,15},{17,16},{18,... | collective-permute-start | bytes 1572872 | tf_op jit(solution)/shard_map/ppermute | solution.py:58
  312.4 35.7 %collective-permute-start.11 = (f32[256,512]{1,0:T(8,128)S(1)}, f32[256,512]{1,0:T(8,128)S(1)}, u32[]{:S(2)}, u32[]{:S(2)}) collective-permute-start(f32[256,512]{1,0:T(8,128)S(1)} %slice_add_fusion.5), channel_id=1, source_target_pairs={{1,0},{2,3},{5,4},{6,7},{9,8},{10,11},{13,12},{14,15},{17,16},{18,... | collective-permute-start | bytes 1572872 | tf_op jit(solution)/shard_map/ppermute | solution.py:58
  336.9 22.5 %collective-permute-start.27 = (f32[256,512]{1,0:T(8,128)S(1)}, f32[256,512]{1,0:T(8,128)S(1)}, u32[]{:S(2)}, u32[]{:S(2)}) collective-permute-start(f32[256,512]{1,0:T(8,128)S(1)} %slice_add_fusion.1), channel_id=1, source_target_pairs={{1,0},{2,3},{5,4},{6,7},{9,8},{10,11},{13,12},{14,15},{17,16},{18,... | collective-permute-start | bytes 1572872 | tf_op jit(solution)/shard_map/ppermute | solution.py:58
  338.7 29.9 %collective-permute-start.31 = (f32[256,512]{1,0:T(8,128)S(1)}, f32[256,512]{1,0:T(8,128)S(1)}, u32[]{:S(2)}, u32[]{:S(2)}) collective-permute-start(f32[256,512]{1,0:T(8,128)S(1)} %slice_add_fusion), channel_id=1, source_target_pairs={{1,0},{2,3},{5,4},{6,7},{9,8},{10,11},{13,12},{14,15},{17,16},{18,... | collective-permute-start | bytes 1572872 | tf_op jit(solution)/shard_map/ppermute | solution.py:58
  348.1 22.9 %collective-permute-start.4 = (f32[128,512]{1,0:T(8,128)S(1)}, f32[128,512]{1,0:T(8,128)S(1)}, u32[]{:S(2)}, u32[]{:S(2)}) collective-permute-start(f32[128,512]{1,0:T(8,128)S(1)} %dynamic-slice_bitcast_fusion.7), channel_id=1, source_target_pairs={{0,8},{8,0},{1,9},{9,1},{2,10},{10,2},{3,11},{11,3},{4,12},{12,4},... | collective-permute-start | bytes 786440 | tf_op jit(solution)/shard_map/ppermute | solution.py:66
  350.2 21.6 %collective-permute-start.8 = (f32[128,512]{1,0:T(8,128)S(1)}, f32[128,512]{1,0:T(8,128)S(1)}, u32[]{:S(2)}, u32[]{:S(2)}) collective-permute-start(f32[128,512]{1,0:T(8,128)S(1)} %dynamic-slice_bitcast_fusion.6), channel_id=1, source_target_pairs={{0,8},{8,0},{1,9},{9,1},{2,10},{10,2},{3,11},{11,3},{4,12},{12,4},... | collective-permute-start | bytes 786440 | tf_op jit(solution)/shard_map/ppermute | solution.py:66
  351.3 22.1 %collective-permute-start.12 = (f32[128,512]{1,0:T(8,128)S(1)}, f32[128,512]{1,0:T(8,128)S(1)}, u32[]{:S(2)}, u32[]{:S(2)}) collective-permute-start(f32[128,512]{1,0:T(8,128)S(1)} %dynamic-slice_bitcast_fusion.5), channel_id=1, source_target_pairs={{0,8},{8,0},{1,9},{9,1},{2,10},{10,2},{3,11},{11,3},{4,12},{12,4},... | collective-permute-start | bytes 786440 | tf_op jit(solution)/shard_map/ppermute | solution.py:66
  359.4 14.7 %collective-permute-start.16 = (f32[128,512]{1,0:T(8,128)S(1)}, f32[128,512]{1,0:T(8,128)S(1)}, u32[]{:S(2)}, u32[]{:S(2)}) collective-permute-start(f32[128,512]{1,0:T(8,128)S(1)} %dynamic-slice_bitcast_fusion.4), channel_id=1, source_target_pairs={{0,8},{8,0},{1,9},{9,1},{2,10},{10,2},{3,11},{11,3},{4,12},{12,4},... | collective-permute-start | bytes 786440 | tf_op jit(solution)/shard_map/ppermute | solution.py:66
  371.1 12.3 %collective-permute-start.24 = (f32[128,512]{1,0:T(8,128)S(1)}, f32[128,512]{1,0:T(8,128)S(1)}, u32[]{:S(2)}, u32[]{:S(2)}) collective-permute-start(f32[128,512]{1,0:T(8,128)S(1)} %dynamic-slice_bitcast_fusion.2), channel_id=1, source_target_pairs={{0,8},{8,0},{1,9},{9,1},{2,10},{10,2},{3,11},{11,3},{4,12},{12,4},... | collective-permute-start | bytes 786440 | tf_op jit(solution)/shard_map/ppermute | solution.py:66
  371.7 17.2 %collective-permute-start.28 = (f32[128,512]{1,0:T(8,128)S(1)}, f32[128,512]{1,0:T(8,128)S(1)}, u32[]{:S(2)}, u32[]{:S(2)}) collective-permute-start(f32[128,512]{1,0:T(8,128)S(1)} %dynamic-slice_bitcast_fusion.1), channel_id=1, source_target_pairs={{0,8},{8,0},{1,9},{9,1},{2,10},{10,2},{3,11},{11,3},{4,12},{12,4},... | collective-permute-start | bytes 786440 | tf_op jit(solution)/shard_map/ppermute | solution.py:66
  373.4 18.4 %collective-permute-start.32 = (f32[128,512]{1,0:T(8,128)S(1)}, f32[128,512]{1,0:T(8,128)S(1)}, u32[]{:S(2)}, u32[]{:S(2)}) collective-permute-start(f32[128,512]{1,0:T(8,128)S(1)} %dynamic-slice_bitcast_fusion), channel_id=1, source_target_pairs={{0,8},{8,0},{1,9},{9,1},{2,10},{10,2},{3,11},{11,3},{4,12},{12,4},... | collective-permute-start | bytes 786440 | tf_op jit(solution)/shard_map/ppermute | solution.py:66
  (12 other events, 64.1 us)
Sparse Core Ops, SparseCore 0:
  8.9 11.7 all-gather.4
  26.0 10.0 all-gather.8
  37.7 34.2 all-gather.6
  73.4 33.0 all-gather.10
where the time goes:
time: 400 us; the launch traced here: 399 us
  waiting for transfers between devices  294 us (74%)
  starting transfers between devices  47.8 us (12%)
  matrix products  29.8 us (7%)
  between operations  14 us (4%)
  local copies, waits for them, and re-layouts  13.4 us (3%)
    ppermute x8, waiting for transfers between devices, on_device(): from_inner = lax.ppermute(to_outer, 'layer', outward)  111 us
    ppermute x8, waiting for transfers between devices, on_device(): theirs = lax.ppermute(mine, 'layer', inward)  90.4 us
    all_gather x2, waiting for transfers between devices, full_dosages(): return lax.all_gather(samples, 'row', axis=1, tiled=True)  53.1 us
    dot_general x40, matrix products, contract(): lax.dot_general(left_rows, right_rows, (((0,), (0,)), ((), ())), preferre...  29.8 us
    ppermute x8, waiting for transfers between devices, on_device(): piece = lax.ppermute(piece, 'row', pairs)  17.4 us
    ppermute x8, starting transfers between devices, on_device(): theirs = lax.ppermute(mine, 'layer', inward)  17.1 us
    ppermute x1, waiting for transfers between devices, on_device(): dosages_in = lax.ppermute(dosages, 'layer', inward)  11.4 us
    ppermute x8, starting transfers between devices, on_device(): from_inner = lax.ppermute(to_outer, 'layer', outward)  10.3 us
  transfers between devices with their start and end apart: 37, of which 18 were waited for; matrix products, arithmetic and copies ran while one was open for 10% of the time, Pallas kernels for 0%

commit v1 on v0

--- a/solution.py
+++ b/solution.py
@@ -12,7 +12,9 @@
 
 
 def full_dosages(local):
-    samples = lax.all_gather(local, "col", axis=0, tiled=True)
+    samples = jnp.concatenate(
+        lax.all_to_all(jnp.stack([local] * lax.axis_size("col")), "col", 0, 0), axis=0
+    )
     return lax.all_gather(samples, "row", axis=1, tiled=True)
 
 

time: 400 us -> 426 us (1.065)
  waiting for transfers between devices: 294 us -> 306 us
  blocking collectives: 0 us -> 9.15 us
    all_gather x2, waiting for transfers between devices: 53.1 us -> 30.1 us  [full_dosages(): return lax.all_gather(samples, 'row', axis=1, tiled=True)]
    ppermute x8, waiting for transfers between devices: 90.4 us -> 110 us  [on_device(): theirs = lax.ppermute(mine, 'layer', inward)]
    ppermute x8, waiting for transfers between devices: 111 us -> 129 us  [on_device(): from_inner = lax.ppermute(to_outer, 'layer', outward)]
    all_gather x2 -> x0, waiting for transfers between devices: 9.45 us -> none  [full_dosages(): samples = lax.all_gather(local, 'col', axis=0, tiled=True)]
    all_to_all x0 -> x2, blocking collectives: none -> 9.15 us  [full_dosages(): lax.all_to_all(jnp.stack([local] * lax.axis_size('col')), 'col', 0, 0)]
    ppermute x8, waiting for transfers between devices: 17.4 us -> 24.9 us  [on_device(): piece = lax.ppermute(piece, 'row', pairs)]
  transfers between devices with their start and end apart: 37 -> 35, of which waited for: 18 -> 19; matrix products, arithmetic and copies ran while one was open for 10% -> 10% of each run, Pallas kernels for 0% -> 0%
where the time goes in v1:
time: 426 us; the launch traced here: 425 us
  waiting for transfers between devices  306 us (72%)
  starting transfers between devices  51.7 us (12%)
  matrix products  29.8 us (7%)
  between operations  14.3 us (3%)
  local copies, waits for them, and re-layouts  13.2 us (3%)
  blocking collectives  9.15 us (2%)
    ppermute x8, waiting for transfers between devices, on_device(): from_inner = lax.ppermute(to_outer, 'layer', outward)  129 us
    ppermute x8, waiting for transfers between devices, on_device(): theirs = lax.ppermute(mine, 'layer', inward)  110 us
    all_gather x2, waiting for transfers between devices, full_dosages(): return lax.all_gather(samples, 'row', axis=1, tiled=True)  30.1 us
    dot_general x40, matrix products, contract(): lax.dot_general(left_rows, right_rows, (((0,), (0,)), ((), ())), preferre...  29.8 us
    ppermute x8, waiting for transfers between devices, on_device(): piece = lax.ppermute(piece, 'row', pairs)  24.9 us
    ppermute x8, starting transfers between devices, on_device(): theirs = lax.ppermute(mine, 'layer', inward)  21 us
    ppermute x1, waiting for transfers between devices, on_device(): dosages_in = lax.ppermute(dosages, 'layer', inward)  11.4 us
    ppermute x8, starting transfers between devices, on_device(): from_inner = lax.ppermute(to_outer, 'layer', outward)  10.3 us
  transfers between devices with their start and end apart: 35, of which 19 were waited for; matrix products, arithmetic and copies ran while one was open for 10% of the time, Pallas kernels for 0%

profile of v1, /device:TPU:0, one launch (start us, length us, event | category | flops | bytes accessed | tf_op | source)
XLA Modules:
  0.0 425.1 jit_solution(17946598774824707199)
XLA Ops:
  7.9 4.6 %all_to_all.10 = bf16[2,512,512]{2,1,0:T(8,128)(2,1)S(1)} all-to-all(bf16[2,512,512]{2,1,0:T(8,128)(2,1)S(1)} %pad_maximum_fusion), channel_id=1, replica_groups=mesh['parts'=2,'row'=2,'col'=2,'layer'=4] {'col'}, dimensions={0} | all-to-all | bytes 2097152 | tf_op jit(solution)/shard_map/all_to_all | solution.py:16
  13.9 5.0 %collective-permute-start = (bf16[512,512]{1,0:T(8,128)(2,1)S(1)}, bf16[512,512]{1,0:T(8,128)(2,1)S(1)}, u32[]{:S(2)}, u32[]{:S(2)}) collective-permute-start(bf16[512,512]{1,0:T(8,128)(2,1)S(1)} %copy-done.4), channel_id=1, source_target_pairs={{0,1},{3,2},{4,5},{7,6},{8,9},{11,10},{12,13},{15,14},{16,17},{19,... | collective-permute-start | bytes 1572872 | tf_op jit(solution)/shard_map/ppermute | solution.py:38
  18.9 11.4 %collective-permute-done = bf16[512,512]{1,0:T(8,128)(2,1)S(1)} collective-permute-done((bf16[512,512]{1,0:T(8,128)(2,1)S(1)}, bf16[512,512]{1,0:T(8,128)(2,1)S(1)}, u32[]{:S(2)}, u32[]{:S(2)}) %collective-permute-start) | collective-permute-done | bytes 524320 | tf_op jit(solution)/shard_map/ppermute | solution.py:38
  30.4 4.6 %all_to_all.11 = bf16[2,512,512]{2,1,0:T(8,128)(2,1)S(1)} all-to-all(bf16[2,512,512]{2,1,0:T(8,128)(2,1)S(1)} %pad_maximum_fusion.1), channel_id=1, replica_groups=mesh['parts'=2,'row'=2,'col'=2,'layer'=4] {'col'}, dimensions={0} | all-to-all | bytes 2097152 | tf_op jit(solution)/shard_map/all_to_all | solution.py:16
  36.3 6.3 %fusion.88 = (bf16[1024,512]{1,0:T(8,128)(2,1)}, bf16[1024,512]{1,0:T(8,128)(2,1)}, bf16[1024,512]{1,0:T(8,128)(2,1)}, bf16[1024,512]{1,0:T(8,128)(2,1)}, bf16[1...) fusion(bf16[1024,4096]{1,0:T(8,128)(2,1)} %param.3), kind=kLoop, calls=%fused_computation.131 | loop fusion | bytes 16777216 | tf_op jit(solution)/shard_map/slice | solution.py:55
  42.6 4.5 %collective-permute-start.29 = (bf16[1024,512]{1,0:T(8,128)(2,1)}, bf16[1024,512]{1,0:T(8,128)(2,1)S(1)}, u32[]{:S(2)}, u32[]{:S(2)}) collective-permute-start(bf16[1024,512]{1,0:T(8,128)(2,1)} %get-tuple-element.5), channel_id=1, source_target_pairs={{0,1},{3,2},{4,5},{7,6},{8,9},{11,10},{12,13},{15,14},{16,17},{19,... | collective-permute-start | bytes 3145736 | tf_op jit(solution)/shard_map/ppermute | solution.py:56
  48.4 2.3 collective-permute-start.21
  52.1 2.3 collective-permute-start.13
  54.4 30.1 %all-gather.5.cloned.1.call-done = bf16[1024,1024]{0,1:T(8,128)(2,1)} async-done(((bf16[1024,512]{0,1:T(8,128)(2,1)}), bf16[1024,1024]{0,1:T(8,128)(2,1)}) %all-gather.5.cloned.1.call-update) | async-done | bytes 2097168 | tf_op jit(solution)/shard_map/all_gather | solution.py:18
  84.5 2.5 constant_dynamic-slice_fusion.5
  87.0 2.1 fusion.26
  89.1 1.9 fusion.34
  94.3 3.5 collective-permute-start.9
  100.6 15.1 %collective-permute-done.21 = bf16[1024,512]{1,0:T(8,128)(2,1)} collective-permute-done((bf16[1024,512]{1,0:T(8,128)(2,1)}, bf16[1024,512]{1,0:T(8,128)(2,1)}, u32[]{:S(2)}, u32[]{:S(2)}) %collective-permute-start.21) | collective-permute-done | bytes 1048608 | tf_op jit(solution)/shard_map/ppermute | solution.py:56
  115.8 4.4 %collective-permute-start.1 = (bf16[1024,512]{1,0:T(8,128)(2,1)S(1)}, bf16[1024,512]{1,0:T(8,128)(2,1)S(1)}, u32[]{:S(2)}, u32[]{:S(2)}) collective-permute-start(bf16[1024,512]{1,0:T(8,128)(2,1)S(1)} %copy-done.1), channel_id=1, source_target_pairs={{0,1},{3,2},{4,5},{7,6},{8,9},{11,10},{12,13},{15,14},{16,17},{19,... | collective-permute-start | bytes 3145736 | tf_op jit(solution)/shard_map/ppermute | solution.py:56
  120.2 1.9 convolution_add_fusion.2
  122.2 16.1 %collective-permute-done.17 = bf16[1024,512]{1,0:T(8,128)(2,1)S(1)} collective-permute-done((bf16[1024,512]{1,0:T(8,128)(2,1)}, bf16[1024,512]{1,0:T(8,128)(2,1)S(1)}, u32[]{:S(2)}, u32[]{:S(2)}) %collective-permute-start.17) | collective-permute-done | bytes 1048608 | tf_op jit(solution)/shard_map/ppermute | solution.py:56
  142.6 18.2 %collective-permute-done.13 = bf16[1024,512]{1,0:T(8,128)(2,1)} collective-permute-done((bf16[1024,512]{1,0:T(8,128)(2,1)}, bf16[1024,512]{1,0:T(8,128)(2,1)}, u32[]{:S(2)}, u32[]{:S(2)}) %collective-permute-start.13) | collective-permute-done | bytes 1048608 | tf_op jit(solution)/shard_map/ppermute | solution.py:56
  161.4 1.9 convolution_add_fusion.4
  163.4 19.7 %collective-permute-done.9 = bf16[1024,512]{1,0:T(8,128)(2,1)S(1)} collective-permute-done((bf16[1024,512]{1,0:T(8,128)(2,1)S(1)}, bf16[1024,512]{1,0:T(8,128)(2,1)S(1)}, u32[]{:S(2)}, u32[]{:S(2)}) %collective-permute-start.9) | collective-permute-done | bytes 1048608 | tf_op jit(solution)/shard_map/ppermute | solution.py:56
  184.7 20.9 %collective-permute-done.5 = bf16[1024,512]{1,0:T(8,128)(2,1)S(1)} collective-permute-done((bf16[1024,512]{1,0:T(8,128)(2,1)S(1)}, bf16[1024,512]{1,0:T(8,128)(2,1)S(1)}, u32[]{:S(2)}, u32[]{:S(2)}) %collective-permute-start.5) | collective-permute-done | bytes 1048608 | tf_op jit(solution)/shard_map/ppermute | solution.py:56
  207.0 20.2 %collective-permute-done.1 = bf16[1024,512]{1,0:T(8,128)(2,1)S(1)} collective-permute-done((bf16[1024,512]{1,0:T(8,128)(2,1)S(1)}, bf16[1024,512]{1,0:T(8,128)(2,1)S(1)}, u32[]{:S(2)}, u32[]{:S(2)}) %collective-permute-start.1) | collective-permute-done | bytes 1048608 | tf_op jit(solution)/shard_map/ppermute | solution.py:56
  242.8 98.1 %collective-permute-done.7 = f32[256,512]{1,0:T(8,128)S(1)} collective-permute-done((f32[256,512]{1,0:T(8,128)S(1)}, f32[256,512]{1,0:T(8,128)S(1)}, u32[]{:S(2)}, u32[]{:S(2)}) %collective-permute-start.7) | collective-permute-done | bytes 524320 | tf_op jit(solution)/shard_map/ppermute | solution.py:60
  342.7 9.5 %collective-permute-done.3 = f32[256,512]{1,0:T(8,128)S(1)} collective-permute-done((f32[256,512]{1,0:T(8,128)S(1)}, f32[256,512]{1,0:T(8,128)S(1)}, u32[]{:S(2)}, u32[]{:S(2)}) %collective-permute-start.3) | collective-permute-done | bytes 524320 | tf_op jit(solution)/shard_map/ppermute | solution.py:60
  354.0 9.4 %collective-permute-done.15 = f32[256,512]{1,0:T(8,128)S(1)} collective-permute-done((f32[256,512]{1,0:T(8,128)S(1)}, f32[256,512]{1,0:T(8,128)S(1)}, u32[]{:S(2)}, u32[]{:S(2)}) %collective-permute-start.15) | collective-permute-done | bytes 524320 | tf_op jit(solution)/shard_map/ppermute | solution.py:60
  366.4 8.2 %collective-permute-done.11 = f32[256,512]{1,0:T(8,128)S(1)} collective-permute-done((f32[256,512]{1,0:T(8,128)S(1)}, f32[256,512]{1,0:T(8,128)S(1)}, u32[]{:S(2)}, u32[]{:S(2)}) %collective-permute-start.11) | collective-permute-done | bytes 524320 | tf_op jit(solution)/shard_map/ppermute | solution.py:60
  379.0 3.8 collective-permute-done.19
  393.5 4.1 collective-permute-done.16
  397.7 5.6 %collective-permute-done.20 = f32[128,512]{1,0:T(8,128)S(1)} collective-permute-done((f32[128,512]{1,0:T(8,128)S(1)}, f32[128,512]{1,0:T(8,128)S(1)}, u32[]{:S(2)}, u32[]{:S(2)}) %collective-permute-start.20) | collective-permute-done | bytes 262176 | tf_op jit(solution)/shard_map/ppermute | solution.py:68
  403.3 5.6 %collective-permute-done.24 = f32[128,512]{1,0:T(8,128)S(1)} collective-permute-done((f32[128,512]{1,0:T(8,128)S(1)}, f32[128,512]{1,0:T(8,128)S(1)}, u32[]{:S(2)}, u32[]{:S(2)}) %collective-permute-start.24) | collective-permute-done | bytes 262176 | tf_op jit(solution)/shard_map/ppermute | solution.py:68
  408.9 5.6 %collective-permute-done.28 = f32[128,512]{1,0:T(8,128)S(1)} collective-permute-done((f32[128,512]{1,0:T(8,128)S(1)}, f32[128,512]{1,0:T(8,128)S(1)}, u32[]{:S(2)}, u32[]{:S(2)}) %collective-permute-start.28) | collective-permute-done | bytes 262176 | tf_op jit(solution)/shard_map/ppermute | solution.py:68
  414.5 3.0 collective-permute-done.32
  (128 shorter events, 58.6 us)
Async XLA Ops:
  6.5 47.8 %all-gather.3.cloned.1.call-start = ((), (), s32[]{:S(2)}) async-start(), calls=%async_computation.2 | async-start | bytes 3145728 | tf_op jit(solution)/shard_map/all_gather | solution.py:18
  13.8 70.6 %all-gather.5.cloned.1.call-start = ((), (), s32[]{:S(2)}) async-start(), calls=%async_computation.3 | async-start | bytes 3145728 | tf_op jit(solution)/shard_map/all_gather | solution.py:18
  13.9 16.4 %collective-permute-start = (bf16[512,512]{1,0:T(8,128)(2,1)S(1)}, bf16[512,512]{1,0:T(8,128)(2,1)S(1)}, u32[]{:S(2)}, u32[]{:S(2)}) collective-permute-start(bf16[512,512]{1,0:T(8,128)(2,1)S(1)} %copy-done.4), channel_id=1, source_target_pairs={{0,1},{3,2},{4,5},{7,6},{8,9},{11,10},{12,13},{15,14},{16,17},{19,... | collective-permute-start | bytes 1572872 | tf_op jit(solution)/shard_map/ppermute | solution.py:38
  42.6 51.7 %collective-permute-start.29 = (bf16[1024,512]{1,0:T(8,128)(2,1)}, bf16[1024,512]{1,0:T(8,128)(2,1)S(1)}, u32[]{:S(2)}, u32[]{:S(2)}) collective-permute-start(bf16[1024,512]{1,0:T(8,128)(2,1)} %get-tuple-element.5), channel_id=1, source_target_pairs={{0,1},{3,2},{4,5},{7,6},{8,9},{11,10},{12,13},{15,14},{16,17},{19,... | collective-permute-start | bytes 3145736 | tf_op jit(solution)/shard_map/ppermute | solution.py:56
  47.1 51.5 %collective-permute-start.25 = (bf16[1024,512]{1,0:T(8,128)(2,1)}, bf16[1024,512]{1,0:T(8,128)(2,1)S(1)}, u32[]{:S(2)}, u32[]{:S(2)}) collective-permute-start(bf16[1024,512]{1,0:T(8,128)(2,1)} %get-tuple-element.12), channel_id=1, source_target_pairs={{0,1},{3,2},{4,5},{7,6},{8,9},{11,10},{12,13},{15,14},{16,17},{19,... | collective-permute-start | bytes 3145736 | tf_op jit(solution)/shard_map/ppermute | solution.py:56
  48.4 67.4 %collective-permute-start.21 = (bf16[1024,512]{1,0:T(8,128)(2,1)}, bf16[1024,512]{1,0:T(8,128)(2,1)}, u32[]{:S(2)}, u32[]{:S(2)}) collective-permute-start(bf16[1024,512]{1,0:T(8,128)(2,1)} %get-tuple-element.6), channel_id=1, source_target_pairs={{0,1},{3,2},{4,5},{7,6},{8,9},{11,10},{12,13},{15,14},{16,17},{19,... | collective-permute-start | bytes 3145736 | tf_op jit(solution)/shard_map/ppermute | solution.py:56
  50.7 87.5 %collective-permute-start.17 = (bf16[1024,512]{1,0:T(8,128)(2,1)}, bf16[1024,512]{1,0:T(8,128)(2,1)S(1)}, u32[]{:S(2)}, u32[]{:S(2)}) collective-permute-start(bf16[1024,512]{1,0:T(8,128)(2,1)} %get-tuple-element.7), channel_id=1, source_target_pairs={{0,1},{3,2},{4,5},{7,6},{8,9},{11,10},{12,13},{15,14},{16,17},{19,... | collective-permute-start | bytes 3145736 | tf_op jit(solution)/shard_map/ppermute | solution.py:56
  52.1 108.6 %collective-permute-start.13 = (bf16[1024,512]{1,0:T(8,128)(2,1)}, bf16[1024,512]{1,0:T(8,128)(2,1)}, u32[]{:S(2)}, u32[]{:S(2)}) collective-permute-start(bf16[1024,512]{1,0:T(8,128)(2,1)} %get-tuple-element.8), channel_id=1, source_target_pairs={{0,1},{3,2},{4,5},{7,6},{8,9},{11,10},{12,13},{15,14},{16,17},{19,... | collective-permute-start | bytes 3145736 | tf_op jit(solution)/shard_map/ppermute | solution.py:56
  94.3 88.7 %collective-permute-start.9 = (bf16[1024,512]{1,0:T(8,128)(2,1)S(1)}, bf16[1024,512]{1,0:T(8,128)(2,1)S(1)}, u32[]{:S(2)}, u32[]{:S(2)}) collective-permute-start(bf16[1024,512]{1,0:T(8,128)(2,1)S(1)} %copy-done.3), channel_id=1, source_target_pairs={{0,1},{3,2},{4,5},{7,6},{8,9},{11,10},{12,13},{15,14},{16,17},{19,... | collective-permute-start | bytes 3145736 | tf_op jit(solution)/shard_map/ppermute | solution.py:56
  98.6 107.0 %collective-permute-start.5 = (bf16[1024,512]{1,0:T(8,128)(2,1)S(1)}, bf16[1024,512]{1,0:T(8,128)(2,1)S(1)}, u32[]{:S(2)}, u32[]{:S(2)}) collective-permute-start(bf16[1024,512]{1,0:T(8,128)(2,1)S(1)} %copy-done.2), channel_id=1, source_target_pairs={{0,1},{3,2},{4,5},{7,6},{8,9},{11,10},{12,13},{15,14},{16,17},{19,... | collective-permute-start | bytes 3145736 | tf_op jit(solution)/shard_map/ppermute | solution.py:56
  115.8 111.4 %collective-permute-start.1 = (bf16[1024,512]{1,0:T(8,128)(2,1)S(1)}, bf16[1024,512]{1,0:T(8,128)(2,1)S(1)}, u32[]{:S(2)}, u32[]{:S(2)}) collective-permute-start(bf16[1024,512]{1,0:T(8,128)(2,1)S(1)} %copy-done.1), channel_id=1, source_target_pairs={{0,1},{3,2},{4,5},{7,6},{8,9},{11,10},{12,13},{15,14},{16,17},{19,... | collective-permute-start | bytes 3145736 | tf_op jit(solution)/shard_map/ppermute | solution.py:56
  141.8 88.6 %collective-permute-start.30 = (f32[512,512]{1,0:T(8,128)S(1)}, f32[512,512]{1,0:T(8,128)S(1)}, u32[]{:S(2)}, u32[]{:S(2)}) collective-permute-start(f32[512,512]{1,0:T(8,128)S(1)} %convolution_add_fusion), channel_id=1, source_target_pairs={{1,2},{2,1},{5,6},{6,5},{9,10},{10,9},{13,14},{14,13},{17,18},{18,... | collective-permute-start | bytes 3145736 | tf_op jit(solution)/shard_map/ppermute | solution.py:58
  160.7 70.9 %collective-permute-start.26 = (f32[512,512]{1,0:T(8,128)S(1)}, f32[512,512]{1,0:T(8,128)S(1)}, u32[]{:S(2)}, u32[]{:S(2)}) collective-permute-start(f32[512,512]{1,0:T(8,128)S(1)} %convolution_add_fusion.1), channel_id=1, source_target_pairs={{1,2},{2,1},{5,6},{6,5},{9,10},{10,9},{13,14},{14,13},{17,18},{18,... | collective-permute-start | bytes 3145736 | tf_op jit(solution)/shard_map/ppermute | solution.py:58
  183.1 49.7 %collective-permute-start.22 = (f32[512,512]{1,0:T(8,128)S(1)}, f32[512,512]{1,0:T(8,128)S(1)}, u32[]{:S(2)}, u32[]{:S(2)}) collective-permute-start(f32[512,512]{1,0:T(8,128)S(1)} %convolution_add_fusion.2), channel_id=1, source_target_pairs={{1,2},{2,1},{5,6},{6,5},{9,10},{10,9},{13,14},{14,13},{17,18},{18,... | collective-permute-start | bytes 3145736 | tf_op jit(solution)/shard_map/ppermute | solution.py:58
  205.6 28.5 %collective-permute-start.18 = (f32[512,512]{1,0:T(8,128)S(1)}, f32[512,512]{1,0:T(8,128)S(1)}, u32[]{:S(2)}, u32[]{:S(2)}) collective-permute-start(f32[512,512]{1,0:T(8,128)S(1)} %convolution_add_fusion.3), channel_id=1, source_target_pairs={{1,2},{2,1},{5,6},{6,5},{9,10},{10,9},{13,14},{14,13},{17,18},{18,... | collective-permute-start | bytes 3145736 | tf_op jit(solution)/shard_map/ppermute | solution.py:58
  230.4 10.6 %collective-permute-start.10 = (f32[512,512]{1,0:T(8,128)S(1)}, f32[512,512]{1,0:T(8,128)S(1)}, u32[]{:S(2)}, u32[]{:S(2)}) collective-permute-start(f32[512,512]{1,0:T(8,128)S(1)} %convolution_add_fusion.5), channel_id=1, source_target_pairs={{1,2},{2,1},{5,6},{6,5},{9,10},{10,9},{13,14},{14,13},{17,18},{18,... | collective-permute-start | bytes 3145736 | tf_op jit(solution)/shard_map/ppermute | solution.py:58
  234.0 150.8 %collective-permute-start.31 = (f32[256,512]{1,0:T(8,128)S(1)}, f32[256,512]{1,0:T(8,128)S(1)}, u32[]{:S(2)}, u32[]{:S(2)}) collective-permute-start(f32[256,512]{1,0:T(8,128)S(1)} %slice_add_fusion), channel_id=1, source_target_pairs={{1,0},{2,3},{5,4},{6,7},{9,8},{10,11},{13,12},{14,15},{17,16},{18,... | collective-permute-start | bytes 1572872 | tf_op jit(solution)/shard_map/ppermute | solution.py:60
  235.8 150.2 %collective-permute-start.27 = (f32[256,512]{1,0:T(8,128)S(1)}, f32[256,512]{1,0:T(8,128)S(1)}, u32[]{:S(2)}, u32[]{:S(2)}) collective-permute-start(f32[256,512]{1,0:T(8,128)S(1)} %slice_add_fusion.1), channel_id=1, source_target_pairs={{1,0},{2,3},{5,4},{6,7},{9,8},{10,11},{13,12},{14,15},{17,16},{18,... | collective-permute-start | bytes 1572872 | tf_op jit(solution)/shard_map/ppermute | solution.py:60
  237.5 139.2 %collective-permute-start.23 = (f32[256,512]{1,0:T(8,128)S(1)}, f32[256,512]{1,0:T(8,128)S(1)}, u32[]{:S(2)}, u32[]{:S(2)}) collective-permute-start(f32[256,512]{1,0:T(8,128)S(1)} %slice_add_fusion.2), channel_id=1, source_target_pairs={{1,0},{2,3},{5,4},{6,7},{9,8},{10,11},{13,12},{14,15},{17,16},{18,... | collective-permute-start | bytes 1572872 | tf_op jit(solution)/shard_map/ppermute | solution.py:60
  239.3 101.6 %collective-permute-start.7 = (f32[256,512]{1,0:T(8,128)S(1)}, f32[256,512]{1,0:T(8,128)S(1)}, u32[]{:S(2)}, u32[]{:S(2)}) collective-permute-start(f32[256,512]{1,0:T(8,128)S(1)} %slice_add_fusion.6), channel_id=1, source_target_pairs={{1,0},{2,3},{5,4},{6,7},{9,8},{10,11},{13,12},{14,15},{17,16},{18,... | collective-permute-start | bytes 1572872 | tf_op jit(solution)/shard_map/ppermute | solution.py:60
  241.1 111.1 %collective-permute-start.3 = (f32[256,512]{1,0:T(8,128)S(1)}, f32[256,512]{1,0:T(8,128)S(1)}, u32[]{:S(2)}, u32[]{:S(2)}) collective-permute-start(f32[256,512]{1,0:T(8,128)S(1)} %slice_add_fusion.7), channel_id=1, source_target_pairs={{1,0},{2,3},{5,4},{6,7},{9,8},{10,11},{13,12},{14,15},{17,16},{18,... | collective-permute-start | bytes 1572872 | tf_op jit(solution)/shard_map/ppermute | solution.py:60
  340.9 22.5 %collective-permute-start.15 = (f32[256,512]{1,0:T(8,128)S(1)}, f32[256,512]{1,0:T(8,128)S(1)}, u32[]{:S(2)}, u32[]{:S(2)}) collective-permute-start(f32[256,512]{1,0:T(8,128)S(1)} %slice_add_fusion.4), channel_id=1, source_target_pairs={{1,0},{2,3},{5,4},{6,7},{9,8},{10,11},{13,12},{14,15},{17,16},{18,... | collective-permute-start | bytes 1572872 | tf_op jit(solution)/shard_map/ppermute | solution.py:60
  352.2 22.5 %collective-permute-start.11 = (f32[256,512]{1,0:T(8,128)S(1)}, f32[256,512]{1,0:T(8,128)S(1)}, u32[]{:S(2)}, u32[]{:S(2)}) collective-permute-start(f32[256,512]{1,0:T(8,128)S(1)} %slice_add_fusion.5), channel_id=1, source_target_pairs={{1,0},{2,3},{5,4},{6,7},{9,8},{10,11},{13,12},{14,15},{17,16},{18,... | collective-permute-start | bytes 1572872 | tf_op jit(solution)/shard_map/ppermute | solution.py:60
  363.4 19.4 %collective-permute-start.19 = (f32[256,512]{1,0:T(8,128)S(1)}, f32[256,512]{1,0:T(8,128)S(1)}, u32[]{:S(2)}, u32[]{:S(2)}) collective-permute-start(f32[256,512]{1,0:T(8,128)S(1)} %slice_add_fusion.3), channel_id=1, source_target_pairs={{1,0},{2,3},{5,4},{6,7},{9,8},{10,11},{13,12},{14,15},{17,16},{18,... | collective-permute-start | bytes 1572872 | tf_op jit(solution)/shard_map/ppermute | solution.py:60
  374.6 13.9 %collective-permute-start.4 = (f32[128,512]{1,0:T(8,128)S(1)}, f32[128,512]{1,0:T(8,128)S(1)}, u32[]{:S(2)}, u32[]{:S(2)}) collective-permute-start(f32[128,512]{1,0:T(8,128)S(1)} %dynamic-slice_bitcast_fusion.7), channel_id=1, source_target_pairs={{0,8},{8,0},{1,9},{9,1},{2,10},{10,2},{3,11},{11,3},{4,12},{12,4},... | collective-permute-start | bytes 786440 | tf_op jit(solution)/shard_map/ppermute | solution.py:68
  376.7 12.5 %collective-permute-start.8 = (f32[128,512]{1,0:T(8,128)S(1)}, f32[128,512]{1,0:T(8,128)S(1)}, u32[]{:S(2)}, u32[]{:S(2)}) collective-permute-start(f32[128,512]{1,0:T(8,128)S(1)} %dynamic-slice_bitcast_fusion.6), channel_id=1, source_target_pairs={{0,8},{8,0},{1,9},{9,1},{2,10},{10,2},{3,11},{11,3},{4,12},{12,4},... | collective-permute-start | bytes 786440 | tf_op jit(solution)/shard_map/ppermute | solution.py:68
  382.8 9.2 %collective-permute-start.12 = (f32[128,512]{1,0:T(8,128)S(1)}, f32[128,512]{1,0:T(8,128)S(1)}, u32[]{:S(2)}, u32[]{:S(2)}) collective-permute-start(f32[128,512]{1,0:T(8,128)S(1)} %dynamic-slice_bitcast_fusion.5), channel_id=1, source_target_pairs={{0,8},{8,0},{1,9},{9,1},{2,10},{10,2},{3,11},{11,3},{4,12},{12,4},... | collective-permute-start | bytes 786440 | tf_op jit(solution)/shard_map/ppermute | solution.py:68
  384.9 12.7 %collective-permute-start.16 = (f32[128,512]{1,0:T(8,128)S(1)}, f32[128,512]{1,0:T(8,128)S(1)}, u32[]{:S(2)}, u32[]{:S(2)}) collective-permute-start(f32[128,512]{1,0:T(8,128)S(1)} %dynamic-slice_bitcast_fusion.4), channel_id=1, source_target_pairs={{0,8},{8,0},{1,9},{9,1},{2,10},{10,2},{3,11},{11,3},{4,12},{12,4},... | collective-permute-start | bytes 786440 | tf_op jit(solution)/shard_map/ppermute | solution.py:68
  386.0 17.2 %collective-permute-start.20 = (f32[128,512]{1,0:T(8,128)S(1)}, f32[128,512]{1,0:T(8,128)S(1)}, u32[]{:S(2)}, u32[]{:S(2)}) collective-permute-start(f32[128,512]{1,0:T(8,128)S(1)} %dynamic-slice_bitcast_fusion.3), channel_id=1, source_target_pairs={{0,8},{8,0},{1,9},{9,1},{2,10},{10,2},{3,11},{11,3},{4,12},{12,4},... | collective-permute-start | bytes 786440 | tf_op jit(solution)/shard_map/ppermute | solution.py:68
  388.5 20.3 %collective-permute-start.24 = (f32[128,512]{1,0:T(8,128)S(1)}, f32[128,512]{1,0:T(8,128)S(1)}, u32[]{:S(2)}, u32[]{:S(2)}) collective-permute-start(f32[128,512]{1,0:T(8,128)S(1)} %dynamic-slice_bitcast_fusion.2), channel_id=1, source_target_pairs={{0,8},{8,0},{1,9},{9,1},{2,10},{10,2},{3,11},{11,3},{4,12},{12,4},... | collective-permute-start | bytes 786440 | tf_op jit(solution)/shard_map/ppermute | solution.py:68
  389.2 25.2 %collective-permute-start.28 = (f32[128,512]{1,0:T(8,128)S(1)}, f32[128,512]{1,0:T(8,128)S(1)}, u32[]{:S(2)}, u32[]{:S(2)}) collective-permute-start(f32[128,512]{1,0:T(8,128)S(1)} %dynamic-slice_bitcast_fusion.1), channel_id=1, source_target_pairs={{0,8},{8,0},{1,9},{9,1},{2,10},{10,2},{3,11},{11,3},{4,12},{12,4},... | collective-permute-start | bytes 786440 | tf_op jit(solution)/shard_map/ppermute | solution.py:68
  392.0 25.6 %collective-permute-start.32 = (f32[128,512]{1,0:T(8,128)S(1)}, f32[128,512]{1,0:T(8,128)S(1)}, u32[]{:S(2)}, u32[]{:S(2)}) collective-permute-start(f32[128,512]{1,0:T(8,128)S(1)} %dynamic-slice_bitcast_fusion), channel_id=1, source_target_pairs={{0,8},{8,0},{1,9},{9,1},{2,10},{10,2},{3,11},{11,3},{4,12},{12,4},... | collective-permute-start | bytes 786440 | tf_op jit(solution)/shard_map/ppermute | solution.py:68
  (10 other events, 66.3 us)
Sparse Core Ops, SparseCore 0:
  13.9 35.8 all-gather.2
  51.3 33.0 all-gather.4
